TPU v7x, 512 devices: a whole 4x8x8 slice. The times are simulated.
512 devices in a mesh: req: 128 (over y, z, core), tp: 4 (over x).
Axes of the slice: x: 4, y: 8, z: 8, core: 2. Of those that a mesh axis runs over, the one named last changes fastest.
Arguments:
- tokens: bfloat16 [65536, 1024], P('req', 'tp')
- placement: int32 [16384], P('req'), may hold values from 0 to 16383, as said below
- cache_len: int32 [256], P('req'), may hold values from 0 to 1024, as said below
- w_query: bfloat16 [1024, 1024], P(None, 'tp'), may hold values from -0.1875 to 0.1875
- w_key: bfloat16 [1024, 1024], P(None, 'tp'), may hold values from -0.1875 to 0.1875
- w_value: bfloat16 [1024, 1024], P(None, 'tp'), may hold values from -0.1875 to 0.1875
- w_out: bfloat16 [1024, 1024], P('tp'), may hold values from -0.1875 to 0.1875
- k_cache: bfloat16 [256, 1024, 1024], P('req', None, 'tp'), may hold values from -6 to 6
- v_cache: bfloat16 [256, 1024, 1024], P('req', None, 'tp'), may hold values from -6 to 6
- ln_gain: float32 [1024], replicated, may hold values from 0.1 to 1.9
- ln_bias: float32 [1024], replicated, may hold values from -0.5 to 0.5
Outputs:
- mixed: bfloat16 [65536, 1024], P('req', 'tp')
Inputs may be any that keep to these rules, and one draw needn't show every extreme that they name: `placement`: A permutation of the blocks. Of the 128 blocks that arrive on index s of req, exactly one goes to the owner range of every index t of req, and it lands at owner position t * 128 + s. `cache_len`: some request has exactly 1024 cached positions.
All inputs are finite; a program needn't handle non-finite values.
Results may differ from a plain program's by a relative error of at most 0.014.
The roundings to bfloat16 on the way count: a program that leaves them out, or rounds other values in their place, can miss the bound.
Values may be sent and summed in bfloat16 or wider, within the bound.
No kernel may reach another device: no remote copies, remote signals or barrier semaphores. Data moves between devices by JAX's collectives and lax.ppermute only.
A program may use at most 64 MiB of HBM per device.

v0:
```python
import jax
import jax.numpy as jnp
from jax import lax
from jax.sharding import PartitionSpec as P

D = 1024
HEADS = 16


def head_view(array, head_size):
    return array.reshape(array.shape[0], array.shape[1] // head_size, head_size)


def attend_padded(queries, new_keys, new_values, cache_keys, cache_values, length):
    head_size = D // HEADS
    new_count = queries.shape[0]
    span = cache_keys.shape[0]
    keys_all = head_view(jnp.concatenate([cache_keys, new_keys], 0), head_size)
    values_all = head_view(jnp.concatenate([cache_values, new_values], 0), head_size)
    query_heads = head_view(queries, head_size)
    scores = jnp.einsum(
        "qhd,khd->hqk", query_heads, keys_all, preferred_element_type=jnp.float32
    ) * head_size ** (-0.5)
    key_pos = jnp.arange(span + new_count, dtype=jnp.int32)[None, :]
    query_pos = jnp.arange(new_count, dtype=jnp.int32)[:, None]
    valid = jnp.where(key_pos < span, key_pos < length, key_pos - span <= query_pos)
    scores = jnp.where(valid[None], scores, -jnp.inf)
    top = jnp.max(scores, axis=-1, keepdims=True)
    weight = jnp.where(valid[None], jnp.exp(scores - top), 0.0)
    total = jnp.sum(weight, axis=-1)
    context = jnp.einsum(
        "hqk,khd->qhd", weight.astype(jnp.bfloat16), values_all, preferred_element_type=jnp.float32
    )
    context = context / jnp.transpose(total)[:, :, None]
    return context.reshape(new_count, queries.shape[1]).astype(jnp.bfloat16)


def attend_all(queries, new_keys, new_values, k_cache, v_cache, cache_len):
    request_count = k_cache.shape[0]
    req_shape = (request_count, queries.shape[0] // request_count, queries.shape[1])
    context = lax.map(
        lambda items: attend_padded(*items),
        (
            queries.reshape(req_shape),
            new_keys.reshape(req_shape),
            new_values.reshape(req_shape),
            k_cache,
            v_cache,
            cache_len,
        ),
    )
    return context.reshape(queries.shape)


def project_rows(whole, w_query, w_key, w_value):
    queries = jnp.dot(whole, w_query, preferred_element_type=jnp.float32).astype(jnp.bfloat16)
    new_keys = jnp.dot(whole, w_key, preferred_element_type=jnp.float32).astype(jnp.bfloat16)
    new_values = jnp.dot(whole, w_value, preferred_element_type=jnp.float32).astype(jnp.bfloat16)
    return (queries, new_keys, new_values)


def finish_rows(context, local, w_out, ln_gain, ln_bias):
    row_count, feat_width = local.shape
    partial_sum = jnp.dot(context, w_out, preferred_element_type=jnp.float32)
    attended = lax.psum_scatter(
        partial_sum.astype(jnp.bfloat16), "tp", scatter_dimension=1, tiled=True
    ).astype(jnp.float32)
    summed = local.astype(jnp.float32) + attended
    first_sum, square_sum = lax.psum(
        (jnp.sum(summed, axis=1), jnp.sum(summed * summed, axis=1)), "tp"
    )
    row_mean = first_sum / D
    row_var = square_sum / D - row_mean * row_mean
    offset = lax.axis_index("tp") * feat_width
    gain_part = lax.dynamic_slice_in_dim(ln_gain, offset, feat_width, 0)
    bias_part = lax.dynamic_slice_in_dim(ln_bias, offset, feat_width, 0)
    scaled = (summed - row_mean[:, None]) / jnp.sqrt(row_var[:, None] + 1e-05)
    return (scaled * gain_part + bias_part).astype(jnp.bfloat16)


def shards(
    tokens, placement, cache_len, w_query, w_key, w_value, w_out, k_cache, v_cache, ln_gain, ln_bias
):
    row_count, feat_width = tokens.shape
    block_count = placement.shape[0]
    block_rows = row_count // block_count
    per_peer = block_count // lax.axis_size("req")
    send_slot = placement // block_count * per_peer + placement % per_peer
    send_order = (
        jnp.zeros((block_count,), jnp.int32)
        .at[send_slot]
        .set(jnp.arange(block_count, dtype=jnp.int32))
    )

    def to_blocks(array):
        return array.reshape(block_count, block_rows, array.shape[1])

    arrived = lax.all_to_all(
        to_blocks(tokens)[send_order], "req", split_axis=0, concat_axis=0, tiled=True
    ).reshape(row_count, feat_width)
    whole = lax.all_gather(arrived, "tp", axis=1, tiled=True)
    queries, new_keys, new_values = project_rows(whole, w_query, w_key, w_value)
    context = attend_all(queries, new_keys, new_values, k_cache, v_cache, cache_len)
    normed = finish_rows(context, arrived, w_out, ln_gain, ln_bias)
    returned = lax.all_to_all(to_blocks(normed), "req", split_axis=0, concat_axis=0, tiled=True)
    return returned[send_slot].reshape(row_count, feat_width)


def solution(mesh):
    in_specs = (
        P("req", "tp"),
        P("req"),
        P("req"),
        P(None, "tp"),
        P(None, "tp"),
        P(None, "tp"),
        P("tp", None),
        P("req", None, "tp"),
        P("req", None, "tp"),
        P(),
        P(),
    )
    out_specs = P("req", "tp")
    return jax.shard_map(shards, mesh=mesh, in_specs=in_specs, out_specs=out_specs, check_vma=False)
```

profile of v0, /device:TPU:2, one launch (start us, length us, event | category | flops | bytes accessed | tf_op | source)
XLA Modules:
  0.0 176.9 jit_solution(9790313830979759242)
XLA Ops:
  6.5 0.7 compare_select_fusion.1
  7.3 1.0 scatter_custom_fusion
  8.3 1.0 reshape.143
  9.3 0.8 gather_fusion
  10.1 32.7 %all_to_all.10 = bf16[128,4,256]{2,1,0:T(4,128)(2,1)S(1)} all-to-all(bf16[128,4,256]{2,1,0:T(4,128)(2,1)S(1)} %gather_fusion), channel_id=1, replica_groups=mesh['req'=128,'tp'=4] {'req'}, dimensions={0} | all-to-all | bytes 524288 | tf_op jit(solution)/shard_map/all_to_all | solution.py:98
  42.8 0.8 reshape.144
  43.7 22.3 %all-gather.2.cloned.1.call-done = bf16[512,1024]{1,0:T(8,128)(2,1)} async-done(((bf16[512,256]{1,0:T(8,128)(2,1)}), bf16[512,1024]{1,0:T(8,128)(2,1)}) %all-gather.2.cloned.1.call-update) | async-done | bytes 1048592 | tf_op jit(solution)/shard_map/all_gather | solution.py:101
  66.0 2.5 %convolution_convert_fusion.2 = bf16[512,256]{1,0:T(8,128)(2,1)} fusion(bf16[512,1024]{1,0:T(8,128)(2,1)} %all-gather.2.cloned.1.call-done, bf16[1024,256]{1,0:T(8,128)(2,1)S(1)} %copy-done.8), kind=kOutput, calls=%fused_computation.43 | convolution fusion | flops 268566528 | bytes 1835008 | tf_op jit(solution)/shard_map/dot_general | solution.py:56
  68.4 1.1 convolution_convert_fusion.1
  69.6 1.1 convolution_convert_fusion.3
  70.8 23.4 %while.12 = (s32[]{:T(128)}, bf16[2,256,256]{2,1,0:T(8,128)(2,1)}, bf16[2,1024,256]{2,1,0:T(8,128)(2,1)S(1)}, bf16[2,256,256]{2,1,0:T(8,128)(2,1)}, s32[2]{0:T(1...) while((s32[]{:T(128)}, bf16[2,256,256]{2,1,0:T(8,128)(2,1)}, ...), condition=%wide.region_4.5_spmd, body=%wide.region_1.4_spmd.sunk | while | flops 521149696 | bytes 12803309 | solution.py:41
  70.8 0.6 dynamic_slice.59
  71.5 0.7 iota_compare_fusion.4
  72.1 0.2 fusion.76
  72.4 1.1 constant_dynamic-slice_fusion.9
  73.5 0.2 copy.40
  73.7 1.0 constant_dynamic-slice_fusion.10
  74.7 0.1 copy.38
  74.9 2.3 %fusion.77 = f32[4,256]{1,0:T(4,128)S(1)} fusion(pred[256,1280]{1,0:T(8,128)(4,1)S(1)} %fusion.76, bf16[256,4,64]{0,2,1:T(8,128)(2,1)S(1)} %bitcast.53, bf16[256,4,64]{0,2,1:T(8,128)(2,1)S(1)} %bitcast.55, bf16[1024,4,64]{0,2,1:T(8,128)(2,1)S(1)} %bitcast.50), kind=kOutput, calls=%fused_computation.7.clone.1 | convolution fusion | flops 175637760 | bytes 1118208 | tf_op jit(solution)/shard_map/while/body/eval_jaxpr/sub | solution.py:29
  77.3 0.2 copy.37
  77.5 0.9 constant_dynamic-slice_fusion.8
  78.5 3.1 %fusion.78 = bf16[256,4,64]{0,2,1:T(8,128)(2,1)S(1)} fusion(pred[256,1280]{1,0:T(8,128)(4,1)S(1)} %fusion.76, bf16[256,4,64]{0,2,1:T(8,128)(2,1)S(1)} %bitcast.57, bf16[1024,4,64]{0,2,1:T(8,128)(2,1)S(1)} %bitcast.52, bf16[256,4,64]{0,2,1:T(8,128)(2,1)} %bitcast.54, bf16[256,4,64]{0,2,1:T(8,128)(2,1)} %bitcast.56, ...), kind=kOutput, calls=%fused_computation.16.clone.1 | convolution fusion | flops 344852736 | bytes 1904640 | tf_op jit(solution)/shard_map/while/body/eval_jaxpr/hqk,khd->qhd/dot_general | solution.py:31
  81.7 0.1 copy.41
  81.8 0.7 copy-done.6
  82.5 0.6 dynamic_slice.59
  83.2 0.7 iota_compare_fusion.4
  83.9 0.2 fusion.76
  84.1 1.1 constant_dynamic-slice_fusion.9
  85.2 0.2 copy.40
  85.4 1.0 constant_dynamic-slice_fusion.10
  86.7 2.3 %fusion.77 = f32[4,256]{1,0:T(4,128)S(1)} fusion(pred[256,1280]{1,0:T(8,128)(4,1)S(1)} %fusion.76, bf16[256,4,64]{0,2,1:T(8,128)(2,1)S(1)} %bitcast.53, bf16[256,4,64]{0,2,1:T(8,128)(2,1)S(1)} %bitcast.55, bf16[1024,4,64]{0,2,1:T(8,128)(2,1)S(1)} %bitcast.50), kind=kOutput, calls=%fused_computation.7.clone.1 | convolution fusion | flops 175637760 | bytes 1118208 | tf_op jit(solution)/shard_map/while/body/eval_jaxpr/sub | solution.py:29
  89.0 0.2 copy.37
  89.2 0.9 constant_dynamic-slice_fusion.8
  90.3 3.1 %fusion.78 = bf16[256,4,64]{0,2,1:T(8,128)(2,1)S(1)} fusion(pred[256,1280]{1,0:T(8,128)(4,1)S(1)} %fusion.76, bf16[256,4,64]{0,2,1:T(8,128)(2,1)S(1)} %bitcast.57, bf16[1024,4,64]{0,2,1:T(8,128)(2,1)S(1)} %bitcast.52, bf16[256,4,64]{0,2,1:T(8,128)(2,1)} %bitcast.54, bf16[256,4,64]{0,2,1:T(8,128)(2,1)} %bitcast.56, ...), kind=kOutput, calls=%fused_computation.16.clone.1 | convolution fusion | flops 344852736 | bytes 1904640 | tf_op jit(solution)/shard_map/while/body/eval_jaxpr/hqk,khd->qhd/dot_general | solution.py:31
  93.4 0.1 copy.41
  93.5 0.7 copy-done.6
  94.2 2.4 %convolution_convert_fusion = bf16[512,1024]{1,0:T(8,128)(2,1)} fusion(bf16[512,256]{1,0:T(8,128)(2,1)} %bitcast.62, bf16[256,1024]{1,0:T(8,128)(2,1)S(1)} %copy-done), kind=kOutput, calls=%fused_computation.41 | convolution fusion | flops 268959744 | bytes 1835008 | tf_op jit(solution)/shard_map/dot_general | solution.py:64
  96.7 0.8 dynamic_slice.45
  97.4 0.8 dynamic_slice.46
  98.2 27.0 %reduce-scatter.2.cloned.1.call-done = bf16[512,256]{1,0:T(8,128)(2,1)} async-done(((bf16[512,1024]{1,0:T(8,128)(2,1)}), bf16[512,256]{1,0:T(8,128)(2,1)}) %reduce-scatter.2.cloned.1.call-update) | async-done | bytes 262160 | tf_op jit(solution)/shard_map/reduce_scatter | solution.py:65
  125.2 1.2 fusion.46
  126.4 10.6 %all-reduce = (f32[512]{0:T(512)S(1)}, f32[512]{0:T(512)S(1)}) all-reduce(f32[512]{0:T(512)S(1)} %get-tuple-element.124, f32[512]{0:T(512)S(1)} %get-tuple-element.123), channel_id=1, replica_groups=mesh['req'=128,'tp'=4] {'tp'}, use_global_device_ids=true, to_apply=%region_9.10 | all-reduce | flops 1024 | bytes 8192 | tf_op jit(solution)/shard_map/psum | solution.py:69
  137.0 1.2 add_convert_fusion
  138.2 0.8 reshape.149
  138.9 14.5 %all-to-all-start.1 = ((bf16[128,4,256]{2,1,0:T(4,128)(2,1)}), bf16[128,4,256]{2,1,0:T(4,128)(2,1)S(1)}, u32[]{:S(2)}, u32[]{:S(2)}) async-start(bf16[128,4,256]{2,1,0:T(4,128)(2,1)} %reshape.149), calls=%async_computation.2 | async-start | bytes 524288 | tf_op jit(solution)/shard_map/all_to_all | solution.py:105
  153.4 15.1 %all-to-all-done.1 = bf16[128,4,256]{2,1,0:T(4,128)(2,1)S(1)} async-done(((bf16[128,4,256]{2,1,0:T(4,128)(2,1)}), bf16[128,4,256]{2,1,0:T(4,128)(2,1)S(1)}, u32[]{:S(2)}, u32[]{:S(2)}) %all-to-all-start.1) | async-done | bytes 262176 | tf_op jit(solution)/shard_map/all_to_all | solution.py:105
  168.5 0.8 gather_fusion.1
  169.3 0.8 reshape.150
  (49 shorter events, 0.8 us)
Async XLA Ops:
  6.5 87.7 %copy-start = (bf16[256,1024]{1,0:T(8,128)(2,1)S(1)}, bf16[256,1024]{1,0:T(8,128)(2,1)}, u32[]{:S(2)}) copy-start(bf16[256,1024]{1,0:T(8,128)(2,1)} %param.19) | copy-start | bytes 1572868
  6.5 59.4 %all-gather.2.cloned.1.call-start = ((), (), s32[]{:S(2)}) async-start(), calls=%async_computation.3 | async-start | bytes 1310720 | tf_op jit(solution)/shard_map/all_gather | solution.py:101
  9.3 56.7 %copy-start.8 = (bf16[1024,256]{1,0:T(8,128)(2,1)S(1)}, bf16[1024,256]{1,0:T(8,128)(2,1)}, u32[]{:S(2)}) copy-start(bf16[1024,256]{1,0:T(8,128)(2,1)} %param.16) | copy-start | bytes 1572868
  43.6 24.8 %copy-start.9 = (bf16[1024,256]{1,0:T(8,128)(2,1)S(1)}, bf16[1024,256]{1,0:T(8,128)(2,1)}, u32[]{:S(2)}) copy-start(bf16[1024,256]{1,0:T(8,128)(2,1)} %param.17) | copy-start | bytes 1572868
  43.6 81.6 %reduce-scatter.2.cloned.1.call-start = ((), (), s32[]{:S(2)}) async-start(), calls=%async_computation.4 | async-start | bytes 1310720 | tf_op jit(solution)/shard_map/reduce_scatter | solution.py:65
  65.9 2.5 %copy-start.7 = (bf16[512,1024]{1,0:T(8,128)(2,1)S(1)}, bf16[512,1024]{1,0:T(8,128)(2,1)}, u32[]{:S(2)}) copy-start(bf16[512,1024]{1,0:T(8,128)(2,1)} %all-gather.2.cloned.1.call-done) | copy-start | bytes 3145732
  68.4 1.1 copy-start.10
  69.6 1.2 copy-start.1
  69.6 1.2 copy-start.11
  74.8 2.5 %copy-start.3 = (bf16[1,256,256]{1,2,0:T(8,128)(2,1)}, bf16[1,256,256]{1,2,0:T(8,128)(2,1)S(1)}, u32[]{:S(2)}) copy-start(bf16[1,256,256]{1,2,0:T(8,128)(2,1)S(1)} %copy.38) | copy-start | bytes 393220 | tf_op jit(solution)/shard_map/while
  74.9 2.3 %copy-start.4 = (bf16[1,256,256]{1,2,0:T(8,128)(2,1)}, bf16[1,256,256]{1,2,0:T(8,128)(2,1)S(1)}, u32[]{:S(2)}) copy-start(bf16[1,256,256]{1,2,0:T(8,128)(2,1)S(1)} %copy.39) | copy-start | bytes 393220 | tf_op jit(solution)/shard_map/while
  78.5 3.3 %copy-start.5 = (bf16[2,256,256]{2,1,0:T(8,128)(2,1)S(1)}, bf16[2,256,256]{2,1,0:T(8,128)(2,1)}, u32[]{:S(2)}) copy-start(bf16[2,256,256]{2,1,0:T(8,128)(2,1)} %get-tuple-element.222) | copy-start | bytes 786436 | tf_op jit(solution)/shard_map/while
  81.8 0.7 copy-start.6
  86.5 2.5 %copy-start.3 = (bf16[1,256,256]{1,2,0:T(8,128)(2,1)}, bf16[1,256,256]{1,2,0:T(8,128)(2,1)S(1)}, u32[]{:S(2)}) copy-start(bf16[1,256,256]{1,2,0:T(8,128)(2,1)S(1)} %copy.38) | copy-start | bytes 393220 | tf_op jit(solution)/shard_map/while
  86.6 2.3 %copy-start.4 = (bf16[1,256,256]{1,2,0:T(8,128)(2,1)}, bf16[1,256,256]{1,2,0:T(8,128)(2,1)S(1)}, u32[]{:S(2)}) copy-start(bf16[1,256,256]{1,2,0:T(8,128)(2,1)S(1)} %copy.39) | copy-start | bytes 393220 | tf_op jit(solution)/shard_map/while
  90.2 3.3 %copy-start.5 = (bf16[2,256,256]{2,1,0:T(8,128)(2,1)S(1)}, bf16[2,256,256]{2,1,0:T(8,128)(2,1)}, u32[]{:S(2)}) copy-start(bf16[2,256,256]{2,1,0:T(8,128)(2,1)} %get-tuple-element.222) | copy-start | bytes 786436 | tf_op jit(solution)/shard_map/while
  93.5 0.7 copy-start.6
  94.2 31.0 %copy-start.2 = (bf16[512,256]{1,0:T(8,128)(2,1)S(1)}, bf16[512,256]{1,0:T(8,128)(2,1)}, u32[]{:S(2)}) copy-start(bf16[512,256]{1,0:T(8,128)(2,1)} %reshape.144) | copy-start | bytes 786436
  138.9 29.6 %all-to-all-start.1 = ((bf16[128,4,256]{2,1,0:T(4,128)(2,1)}), bf16[128,4,256]{2,1,0:T(4,128)(2,1)S(1)}, u32[]{:S(2)}, u32[]{:S(2)}) async-start(bf16[128,4,256]{2,1,0:T(4,128)(2,1)} %reshape.149), calls=%async_computation.2 | async-start | bytes 524288 | tf_op jit(solution)/shard_map/all_to_all | solution.py:105
Sparse Core Ops, SparseCore 0:
  43.7 22.1 all-gather.1
  96.8 28.3 reduce-scatter.1
where the time goes:
time: 178 us; the launch traced here: 177 us
  waiting for transfers between devices  64.4 us (36%)
  blocking collectives  43.3 us (24%)
  matrix products  18.1 us (10%)
  local copies, waits for them, and re-layouts  18 us (10%)
  starting transfers between devices  14.5 us (8%)
  between operations  13.5 us (8%)
  other arithmetic  4.9 us (3%)
    all_to_all x1, blocking collectives, shards(): lax.all_to_all(to_blocks(tokens)[send_order], 'req', split_axis=0, concat...  32.7 us
    reduce_scatter x1, waiting for transfers between devices, finish_rows(): lax.psum_scatter(partial_sum.astype(jnp.bfloat16), 'tp', scatter_dimensio...  27 us
    all_gather x1, waiting for transfers between devices, shards(): whole = lax.all_gather(arrived, 'tp', axis=1, tiled=True)  22.3 us
    all_to_all x1, waiting for transfers between devices, shards(): lax.all_to_all(to_blocks(normed), 'req', split_axis=0, concat_axis=0, til...  15.1 us
    all_to_all x1, starting transfers between devices, shards(): lax.all_to_all(to_blocks(normed), 'req', split_axis=0, concat_axis=0, til...  14.5 us
    psum x1, blocking collectives, finish_rows(): lax.psum((jnp.sum(summed, axis=1), jnp.sum(summed * summed, axis=1)), 'tp')  10.6 us
    dynamic_slice x18, local copies, waits for them, and re-layouts, attend_all(): lax.map(lambda items: attend_padded(*items), (queries.reshape(req_shape),...  8.77 us
    dot_general x2, matrix products, attend_padded(): jnp.einsum('hqk,khd->qhd', weight.astype(jnp.bfloat16), values_all, prefe...  6.26 us
  transfers between devices with their start and end apart: 3, of which 3 were waited for; matrix products, arithmetic and copies ran while one was open for 1% of the time, Pallas kernels for 0%

commit v1 on v0

--- a/solution.py
+++ b/solution.py
@@ -98,7 +98,9 @@
     arrived = lax.all_to_all(
         to_blocks(tokens)[send_order], "req", split_axis=0, concat_axis=0, tiled=True
     ).reshape(row_count, feat_width)
-    whole = lax.all_gather(arrived, "tp", axis=1, tiled=True)
+    whole = jnp.concatenate(
+        lax.all_to_all(jnp.stack([arrived] * lax.axis_size("tp")), "tp", 0, 0), axis=1
+    )
     queries, new_keys, new_values = project_rows(whole, w_query, w_key, w_value)
     context = attend_all(queries, new_keys, new_values, k_cache, v_cache, cache_len)
     normed = finish_rows(context, arrived, w_out, ln_gain, ln_bias)

time: 178 us -> 163 us (0.916)
  waiting for transfers between devices: 64.4 us -> 45.4 us
  starting transfers between devices: 14.5 us -> 19.5 us
    all_gather x1 -> x0, waiting for transfers between devices: 22.3 us -> none  [shards(): whole = lax.all_gather(arrived, 'tp', axis=1, tiled=True)]
    all_to_all x0 -> x1, waiting for transfers between devices: none -> 12.6 us  [shards(): lax.all_to_all(jnp.stack([arrived] * lax.axis_size('tp')), 'tp', 0, 0)]
    reduce_scatter x1, waiting for transfers between devices: 27 us -> 17.7 us  [finish_rows(): lax.psum_scatter(partial_sum.astype(jnp.bfloat16), 'tp', scatter_dimensio...]
    all_to_all x0 -> x1, starting transfers between devices: none -> 4.96 us  [shards(): lax.all_to_all(jnp.stack([arrived] * lax.axis_size('tp')), 'tp', 0, 0)]
where the time goes in v1:
time: 163 us; the launch traced here: 162 us
  waiting for transfers between devices  45.4 us (28%)
  blocking collectives  43.3 us (27%)
  starting transfers between devices  19.5 us (12%)
  local copies, waits for them, and re-layouts  18.4 us (11%)
  matrix products  16.8 us (10%)
  between operations  13.5 us (8%)
  other arithmetic  4.82 us (3%)
    all_to_all x1, blocking collectives, shards(): lax.all_to_all(to_blocks(tokens)[send_order], 'req', split_axis=0, concat...  32.7 us
    reduce_scatter x1, waiting for transfers between devices, finish_rows(): lax.psum_scatter(partial_sum.astype(jnp.bfloat16), 'tp', scatter_dimensio...  17.7 us
    all_to_all x1, waiting for transfers between devices, shards(): lax.all_to_all(to_blocks(normed), 'req', split_axis=0, concat_axis=0, til...  15.1 us
    all_to_all x1, starting transfers between devices, shards(): lax.all_to_all(to_blocks(normed), 'req', split_axis=0, concat_axis=0, til...  14.5 us
    all_to_all x1, waiting for transfers between devices, shards(): lax.all_to_all(jnp.stack([arrived] * lax.axis_size('tp')), 'tp', 0, 0)  12.6 us
    psum x1, blocking collectives, finish_rows(): lax.psum((jnp.sum(summed, axis=1), jnp.sum(summed * summed, axis=1)), 'tp')  10.6 us
    dynamic_slice x18, local copies, waits for them, and re-layouts, attend_all(): lax.map(lambda items: attend_padded(*items), (queries.reshape(req_shape),...  8.68 us
    dot_general x2, matrix products, attend_padded(): jnp.einsum('hqk,khd->qhd', weight.astype(jnp.bfloat16), values_all, prefe...  6.26 us
  transfers between devices with their start and end apart: 3, of which 3 were waited for; matrix products, arithmetic and copies ran while one was open for 1% of the time, Pallas kernels for 0%

profile of v1, /device:TPU:2, one launch (start us, length us, event | category | flops | bytes accessed | tf_op | source)
XLA Modules:
  0.0 162.0 jit_solution(3553267485561983643)
XLA Ops:
  6.5 0.7 compare_select_fusion.1
  7.3 1.0 scatter_custom_fusion
  8.3 1.0 reshape.151
  9.3 0.8 gather_fusion
  10.1 32.7 %all_to_all.15 = bf16[128,4,256]{2,1,0:T(4,128)(2,1)S(1)} all-to-all(bf16[128,4,256]{2,1,0:T(4,128)(2,1)S(1)} %gather_fusion), channel_id=1, replica_groups=mesh['req'=128,'tp'=4] {'req'}, dimensions={0} | all-to-all | bytes 524288 | tf_op jit(solution)/shard_map/all_to_all | solution.py:98
  42.9 0.1 copy.17
  43.1 1.0 stack.3
  44.1 5.0 %all-to-all-start.1 = ((bf16[4,512,256]{1,2,0:T(8,128)(2,1)}), bf16[4,512,256]{1,2,0:T(8,128)(2,1)S(1)}, u32[]{:S(2)}, u32[]{:S(2)}) async-start(bf16[4,512,256]{1,2,0:T(8,128)(2,1)} %stack.3), calls=%async_computation.1 | async-start | bytes 2097152 | tf_op jit(solution)/shard_map/all_to_all | solution.py:102
  49.1 12.6 %all-to-all-done.1 = bf16[4,512,256]{1,2,0:T(8,128)(2,1)S(1)} async-done(((bf16[4,512,256]{1,2,0:T(8,128)(2,1)}), bf16[4,512,256]{1,2,0:T(8,128)(2,1)S(1)}, u32[]{:S(2)}, u32[]{:S(2)}) %all-to-all-start.1) | async-done | bytes 1048608 | tf_op jit(solution)/shard_map/all_to_all | solution.py:102
  61.7 1.2 convolution_convert_fusion.3
  62.9 1.2 convolution_convert_fusion.2
  64.1 1.2 convolution_convert_fusion.1
  65.3 23.3 %while.12 = (s32[]{:T(128)}, bf16[2,256,256]{2,1,0:T(8,128)(2,1)}, bf16[2,1024,256]{2,1,0:T(8,128)(2,1)S(1)}, bf16[2,256,256]{2,1,0:T(8,128)(2,1)}, s32[2]{0:T(1...) while((s32[]{:T(128)}, bf16[2,256,256]{2,1,0:T(8,128)(2,1)}, ...), condition=%wide.region_4.5_spmd, body=%wide.region_1.4_spmd.sunk | while | flops 521149696 | bytes 12803309 | solution.py:41
  65.3 0.6 dynamic_slice.59
  65.9 0.6 iota_compare_fusion.4
  66.6 0.2 fusion.76
  66.8 1.1 constant_dynamic-slice_fusion.9
  67.9 0.2 copy.41
  68.1 1.0 constant_dynamic-slice_fusion.10
  69.4 2.3 %fusion.77 = f32[4,256]{1,0:T(4,128)S(1)} fusion(pred[256,1280]{1,0:T(8,128)(4,1)S(1)} %fusion.76, bf16[256,4,64]{0,2,1:T(8,128)(2,1)S(1)} %bitcast.56, bf16[256,4,64]{0,2,1:T(8,128)(2,1)S(1)} %bitcast.58, bf16[1024,4,64]{0,2,1:T(8,128)(2,1)S(1)} %bitcast.53), kind=kOutput, calls=%fused_computation.7.clone.1 | convolution fusion | flops 175637760 | bytes 1118208 | tf_op jit(solution)/shard_map/while/body/eval_jaxpr/sub | solution.py:29
  71.7 0.2 copy.38
  71.9 0.9 constant_dynamic-slice_fusion.8
  73.0 3.1 %fusion.78 = bf16[256,4,64]{0,2,1:T(8,128)(2,1)S(1)} fusion(pred[256,1280]{1,0:T(8,128)(4,1)S(1)} %fusion.76, bf16[256,4,64]{0,2,1:T(8,128)(2,1)S(1)} %bitcast.60, bf16[1024,4,64]{0,2,1:T(8,128)(2,1)S(1)} %bitcast.55, bf16[256,4,64]{0,2,1:T(8,128)(2,1)} %bitcast.57, bf16[256,4,64]{0,2,1:T(8,128)(2,1)} %bitcast.59, ...), kind=kOutput, calls=%fused_computation.16.clone.1 | convolution fusion | flops 344852736 | bytes 1904640 | tf_op jit(solution)/shard_map/while/body/eval_jaxpr/hqk,khd->qhd/dot_general | solution.py:31
  76.2 0.7 copy-done.7
  76.9 0.6 dynamic_slice.59
  77.5 0.6 iota_compare_fusion.4
  78.2 0.2 fusion.76
  78.4 1.1 constant_dynamic-slice_fusion.9
  79.6 0.2 copy.41
  79.8 1.0 constant_dynamic-slice_fusion.10
  81.0 2.3 %fusion.77 = f32[4,256]{1,0:T(4,128)S(1)} fusion(pred[256,1280]{1,0:T(8,128)(4,1)S(1)} %fusion.76, bf16[256,4,64]{0,2,1:T(8,128)(2,1)S(1)} %bitcast.56, bf16[256,4,64]{0,2,1:T(8,128)(2,1)S(1)} %bitcast.58, bf16[1024,4,64]{0,2,1:T(8,128)(2,1)S(1)} %bitcast.53), kind=kOutput, calls=%fused_computation.7.clone.1 | convolution fusion | flops 175637760 | bytes 1118208 | tf_op jit(solution)/shard_map/while/body/eval_jaxpr/sub | solution.py:29
  83.3 0.2 copy.38
  83.6 0.9 constant_dynamic-slice_fusion.8
  84.6 3.1 %fusion.78 = bf16[256,4,64]{0,2,1:T(8,128)(2,1)S(1)} fusion(pred[256,1280]{1,0:T(8,128)(4,1)S(1)} %fusion.76, bf16[256,4,64]{0,2,1:T(8,128)(2,1)S(1)} %bitcast.60, bf16[1024,4,64]{0,2,1:T(8,128)(2,1)S(1)} %bitcast.55, bf16[256,4,64]{0,2,1:T(8,128)(2,1)} %bitcast.57, bf16[256,4,64]{0,2,1:T(8,128)(2,1)} %bitcast.59, ...), kind=kOutput, calls=%fused_computation.16.clone.1 | convolution fusion | flops 344852736 | bytes 1904640 | tf_op jit(solution)/shard_map/while/body/eval_jaxpr/hqk,khd->qhd/dot_general | solution.py:31
  87.7 0.1 copy.42
  87.9 0.7 copy-done.7
  88.6 2.4 %convolution_convert_fusion = bf16[512,1024]{1,0:T(8,128)(2,1)} fusion(bf16[512,256]{1,0:T(8,128)(2,1)} %bitcast.68, bf16[256,1024]{1,0:T(8,128)(2,1)S(1)} %copy-done), kind=kOutput, calls=%fused_computation.41 | convolution fusion | flops 268959744 | bytes 1835008 | tf_op jit(solution)/shard_map/dot_general | solution.py:64
  91.0 0.8 dynamic_slice.45
  91.8 0.8 dynamic_slice.46
  92.5 17.7 %reduce-scatter.2.cloned.1.call-done = bf16[512,256]{1,0:T(8,128)(2,1)} async-done(((bf16[512,1024]{1,0:T(8,128)(2,1)}), bf16[512,256]{1,0:T(8,128)(2,1)}) %reduce-scatter.2.cloned.1.call-update) | async-done | bytes 262160 | tf_op jit(solution)/shard_map/reduce_scatter | solution.py:65
  110.2 1.2 fusion.46
  111.4 10.6 %all-reduce = (f32[512]{0:T(512)S(1)}, f32[512]{0:T(512)S(1)}) all-reduce(f32[512]{0:T(512)S(1)} %get-tuple-element.124, f32[512]{0:T(512)S(1)} %get-tuple-element.123), channel_id=1, replica_groups=mesh['req'=128,'tp'=4] {'tp'}, use_global_device_ids=true, to_apply=%region_9.10 | all-reduce | flops 1024 | bytes 8192 | tf_op jit(solution)/shard_map/psum | solution.py:69
  122.0 1.2 add_convert_fusion
  123.2 0.8 reshape.159
  124.0 14.5 %all-to-all-start.2 = ((bf16[128,4,256]{2,1,0:T(4,128)(2,1)}), bf16[128,4,256]{2,1,0:T(4,128)(2,1)S(1)}, u32[]{:S(2)}, u32[]{:S(2)}) async-start(bf16[128,4,256]{2,1,0:T(4,128)(2,1)} %reshape.159), calls=%async_computation.3 | async-start | bytes 524288 | tf_op jit(solution)/shard_map/all_to_all | solution.py:107
  138.5 15.1 %all-to-all-done.2 = bf16[128,4,256]{2,1,0:T(4,128)(2,1)S(1)} async-done(((bf16[128,4,256]{2,1,0:T(4,128)(2,1)}), bf16[128,4,256]{2,1,0:T(4,128)(2,1)S(1)}, u32[]{:S(2)}, u32[]{:S(2)}) %all-to-all-start.2) | async-done | bytes 262176 | tf_op jit(solution)/shard_map/all_to_all | solution.py:107
  153.6 0.8 gather_fusion.1
  154.4 0.8 reshape.160
  (50 shorter events, 1.0 us)
Async XLA Ops:
  6.5 82.0 %copy-start = (bf16[256,1024]{1,0:T(8,128)(2,1)S(1)}, bf16[256,1024]{1,0:T(8,128)(2,1)}, u32[]{:S(2)}) copy-start(bf16[256,1024]{1,0:T(8,128)(2,1)} %param.19) | copy-start | bytes 1572868
  42.9 1.2 copy-start.2
  44.1 17.6 %copy-start.8 = (bf16[1024,256]{1,0:T(8,128)(2,1)S(1)}, bf16[1024,256]{1,0:T(8,128)(2,1)}, u32[]{:S(2)}) copy-start(bf16[1024,256]{1,0:T(8,128)(2,1)} %param.18) | copy-start | bytes 1572868
  44.1 17.6 %all-to-all-start.1 = ((bf16[4,512,256]{1,2,0:T(8,128)(2,1)}), bf16[4,512,256]{1,2,0:T(8,128)(2,1)S(1)}, u32[]{:S(2)}, u32[]{:S(2)}) async-start(bf16[4,512,256]{1,2,0:T(8,128)(2,1)} %stack.3), calls=%async_computation.1 | async-start | bytes 2097152 | tf_op jit(solution)/shard_map/all_to_all | solution.py:102
  49.1 61.2 %reduce-scatter.2.cloned.1.call-start = ((), (), s32[]{:S(2)}) async-start(), calls=%async_computation.4 | async-start | bytes 1310720 | tf_op jit(solution)/shard_map/reduce_scatter | solution.py:65
  61.7 1.2 copy-start.9
  62.9 1.2 copy-start.10
  64.1 1.2 copy-start.1
  64.1 1.2 copy-start.11
  69.2 2.5 %copy-start.4 = (bf16[1,256,256]{1,2,0:T(8,128)(2,1)}, bf16[1,256,256]{1,2,0:T(8,128)(2,1)S(1)}, u32[]{:S(2)}) copy-start(bf16[1,256,256]{1,2,0:T(8,128)(2,1)S(1)} %copy.39) | copy-start | bytes 393220 | tf_op jit(solution)/shard_map/while
  69.3 2.3 %copy-start.5 = (bf16[1,256,256]{1,2,0:T(8,128)(2,1)}, bf16[1,256,256]{1,2,0:T(8,128)(2,1)S(1)}, u32[]{:S(2)}) copy-start(bf16[1,256,256]{1,2,0:T(8,128)(2,1)S(1)} %copy.40) | copy-start | bytes 393220 | tf_op jit(solution)/shard_map/while
  72.9 3.3 %copy-start.6 = (bf16[2,256,256]{2,1,0:T(8,128)(2,1)S(1)}, bf16[2,256,256]{2,1,0:T(8,128)(2,1)}, u32[]{:S(2)}) copy-start(bf16[2,256,256]{2,1,0:T(8,128)(2,1)} %get-tuple-element.222) | copy-start | bytes 786436 | tf_op jit(solution)/shard_map/while
  76.2 0.7 copy-start.7
  80.9 2.5 %copy-start.4 = (bf16[1,256,256]{1,2,0:T(8,128)(2,1)}, bf16[1,256,256]{1,2,0:T(8,128)(2,1)S(1)}, u32[]{:S(2)}) copy-start(bf16[1,256,256]{1,2,0:T(8,128)(2,1)S(1)} %copy.39) | copy-start | bytes 393220 | tf_op jit(solution)/shard_map/while
  81.0 2.3 %copy-start.5 = (bf16[1,256,256]{1,2,0:T(8,128)(2,1)}, bf16[1,256,256]{1,2,0:T(8,128)(2,1)S(1)}, u32[]{:S(2)}) copy-start(bf16[1,256,256]{1,2,0:T(8,128)(2,1)S(1)} %copy.40) | copy-start | bytes 393220 | tf_op jit(solution)/shard_map/while
  84.6 3.3 %copy-start.6 = (bf16[2,256,256]{2,1,0:T(8,128)(2,1)S(1)}, bf16[2,256,256]{2,1,0:T(8,128)(2,1)}, u32[]{:S(2)}) copy-start(bf16[2,256,256]{2,1,0:T(8,128)(2,1)} %get-tuple-element.222) | copy-start | bytes 786436 | tf_op jit(solution)/shard_map/while
  87.9 0.7 copy-start.7
  88.6 21.7 %copy-start.3 = (bf16[512,256]{1,0:T(8,128)(2,1)S(1)}, bf16[512,256]{1,0:T(8,128)(2,1)}, u32[]{:S(2)}) copy-start(bf16[512,256]{1,0:T(8,128)(2,1)} %copy-done.2) | copy-start | bytes 786436
  124.0 29.6 %all-to-all-start.2 = ((bf16[128,4,256]{2,1,0:T(4,128)(2,1)}), bf16[128,4,256]{2,1,0:T(4,128)(2,1)S(1)}, u32[]{:S(2)}, u32[]{:S(2)}) async-start(bf16[128,4,256]{2,1,0:T(4,128)(2,1)} %reshape.159), calls=%async_computation.3 | async-start | bytes 524288 | tf_op jit(solution)/shard_map/all_to_all | solution.py:107
Sparse Core Ops, SparseCore 0:
  91.1 19.0 reduce-scatter.1
